TPU v7x, 32 devices: a whole 2x2x4 slice. The times are simulated.
32 devices in a mesh: groups: 2 (over x), seq: 8 (over z, y), head: 2 (over core).
Axes of the slice: x: 2, y: 2, z: 4, core: 2. Of those that a mesh axis runs over, the one named last changes fastest.
Arguments:
- x_input: bfloat16 [2048, 4096], P(('groups', 'seq'), 'head'), parts along dimension 0, may hold values from -6 to 6
- b_rows: bfloat16 [2048, 128], P(('groups', 'seq')), parts along dimension 0, may hold values from -0.5 to 0.5
- c_rows: bfloat16 [2048, 128], P(('groups', 'seq')), parts along dimension 0, may hold values from -0.5 to 0.5
- decay_log: float32 [64, 1024], P(('groups', 'head'), 'seq'), parts along dimension 0, may hold values from -1 to 0
- skip_gain: float32 [32], P('head'), may hold values from 0.5 to 1.5
- doc_lengths: int32 [8], P('groups'), parts along dimension 0, may hold values from 1 to 512, 1024 in all
- queries: bfloat16 [2048, 2048], P(('groups', 'seq'), 'head'), parts along dimension 0, may hold values from -9 to 9
- attention_key_rows: bfloat16 [2048, 512], P(('groups', 'seq'), 'head'), parts along dimension 0, may hold values from -9 to 9
- values: bfloat16 [2048, 512], P(('groups', 'seq'), 'head'), parts along dimension 0, may hold values from -6 to 6
- mixer_cot: bfloat16 [2048, 4096], P(('groups', 'seq'), 'head'), parts along dimension 0, may hold values from -6 to 6
- attention_output_cotangent: bfloat16 [2048, 2048], P(('groups', 'seq'), 'head'), parts along dimension 0, may hold values from -6 to 6
Outputs:
- mixer_out: bfloat16 [2048, 4096], P(('groups', 'seq'), 'head'), parts along dimension 0
- attn_out: bfloat16 [2048, 2048], P(('groups', 'seq'), 'head'), parts along dimension 0
- x_grad: bfloat16 [2048, 4096], P(('groups', 'seq'), 'head'), parts along dimension 0
- b_grad: float32 [2048, 128], P(('groups', 'seq')), parts along dimension 0
- c_grad: float32 [2048, 128], P(('groups', 'seq')), parts along dimension 0
- decay_grad: float32 [64, 1024], P(('groups', 'head'), 'seq'), parts along dimension 0
- q_grad: bfloat16 [2048, 2048], P(('groups', 'seq'), 'head'), parts along dimension 0
- key_gradient: bfloat16 [2048, 512], P(('groups', 'seq'), 'head'), parts along dimension 0
- value_gradient: bfloat16 [2048, 512], P(('groups', 'seq'), 'head'), parts along dimension 0
There are 2 independent parts, one for each index of `groups`. A program takes and returns all parts, laid end to end along the dimension named above; an argument that names none is the same for every part. Nothing has to cross between parts.
Inputs may be any that keep to these rules, and one draw needn't show every extreme that they name: `doc_lengths`: the lengths of the documents packed into the stream, in order; they sum to 1024.
All inputs are finite; a program needn't handle non-finite values.
Results may differ from a plain program's by a relative error of at most 0.023.
Values may be sent and summed in bfloat16 or wider, within the bound.
No kernel may reach another device: no remote copies, remote signals or barrier semaphores. Data moves between devices by JAX's collectives and lax.ppermute only.
A program may use at most 128 MiB of HBM per device.

v0:
```python
import math
import jax
import jax.numpy as jnp
from jax import lax
from jax.sharding import PartitionSpec as P

P_SIZE = 128
HEAD_SIZE = 128
TOK_SPAN = 128
precise = lax.Precision.HIGHEST
big_negative = -1e30


def entering_2(part, axis, combine, identity, reverse):
    count = lax.axis_size(axis)
    place = lax.axis_index(axis)
    ahead = count - 1 - place if reverse else place
    early = jax.tree.map(lambda a, e: jnp.zeros_like(a) + jnp.asarray(e, a.dtype), part, identity)
    span = part
    shift = 1
    while shift < count:
        if reverse:
            pairs = [(i, i - shift) for i in range(shift, count)]
        else:
            pairs = [(i, i + shift) for i in range(count - shift)]
        got = lax.ppermute(span, axis, pairs)
        have = ahead >= shift
        got = jax.tree.map(lambda g, e: jnp.where(have, g, jnp.asarray(e, g.dtype)), got, identity)
        early = combine(got, early)
        if 2 * shift < count:
            span = combine(got, span)
        shift *= 2
    return early


def doc_index(positions, lengths):
    ends = jnp.cumsum(lengths)
    return jnp.sum((positions[:, None] >= ends[None, :]).astype(jnp.int32), axis=1)


def cumulate(decay):
    return jnp.cumsum(decay, axis=1)


def local_state(inputs, b_float, cumulated, segment):
    weights = (
        jnp.exp(cumulated[:, -1:] - cumulated)
        * (segment == segment[-1]).astype(inputs.dtype)[None, :]
    )
    return jnp.einsum("hs,sn,shp->hnp", weights, b_float, inputs, precision=precise)


def carry_factor(cumulated, segment, before):
    return jnp.exp(cumulated[:, -1]) * (segment[-1] == before).astype(cumulated.dtype)


def mixer_stretch(inputs, b_float, c_float, decay, gains, segment, before, state_in):
    cumulated = cumulate(decay)
    width = inputs.shape[0]
    steps = jnp.arange(width)
    allowed = (steps[:, None] >= steps[None, :]) & (segment[:, None] == segment[None, :])
    gaps = jnp.where(allowed[None], cumulated[:, :, None] - cumulated[:, None, :], big_negative)
    kernel = jnp.exp(gaps) * jnp.dot(c_float, b_float.T, precision=precise)[None]
    inner = jnp.einsum("hts,shp->thp", kernel, inputs, precision=precise)
    keeps = (segment == before).astype(inputs.dtype)
    entering = jnp.einsum("tn,hnp->thp", c_float, state_in, precision=precise)
    reach = jnp.exp(cumulated).T * keeps[:, None]
    outputs = inner + reach[:, :, None] * entering + gains[None, :, None] * inputs
    factor = carry_factor(cumulated, segment, before)
    state_out = factor[:, None, None] * state_in + local_state(inputs, b_float, cumulated, segment)
    return (outputs, state_out)


def combine_states(earlier, later):
    return (earlier[0] * later[0], later[0][:, None, None] * earlier[1] + later[1])


def mixer_whole(inputs, b_float, c_float, decay, gains, segment):
    width = TOK_SPAN
    count = inputs.shape[0] // width
    heads = inputs.shape[1]
    inp = inputs.reshape(count, width, heads, P_SIZE)
    b_blocks = b_float.reshape(count, width, -1)
    c_blocks = c_float.reshape(count, width, -1)
    dec = decay.reshape(heads, count, width).transpose(1, 0, 2)
    seg = segment.reshape(count, width)
    befores = jnp.concatenate([jnp.full((1,), -1, seg.dtype), seg[:-1, -1]])
    cumulated = jnp.cumsum(dec, axis=2)
    factor = jax.vmap(carry_factor)(cumulated, seg, befores)
    summary = jax.vmap(local_state)(inp, b_blocks, cumulated, seg)

    def advance(carried, pieces):
        fac, summ = pieces
        return (fac[:, None, None] * carried + summ, carried)

    unused, state_in = lax.scan(advance, jnp.zeros_like(summary[0]), (factor, summary))

    def stretch(i, brow, crow, d, sg, bf, st):
        return mixer_stretch(i, brow, crow, d, gains, sg, bf, st)[0]

    outputs = jax.vmap(stretch)(inp, b_blocks, c_blocks, dec, seg, befores, state_in)
    return outputs.reshape(count * width, heads, P_SIZE)


def mamba_by_heads(x_input, b_all, c_all, decay_log, skip_gain, doc_lengths, mixer_cot):
    seq_count = lax.axis_size("seq")
    place = lax.axis_index("seq")
    tokens = x_input.shape[0]
    heads_here = skip_gain.shape[0]
    own = heads_here // seq_count
    total = tokens * seq_count
    pair = lax.all_to_all(
        jnp.stack([x_input, mixer_cot]), "seq", split_axis=2, concat_axis=1, tiled=True
    )
    decay = lax.all_to_all(decay_log, "seq", split_axis=0, concat_axis=1, tiled=True)
    gains = lax.dynamic_slice_in_dim(skip_gain, place * own, own)
    segment = doc_index(jnp.arange(total, dtype=jnp.int32), doc_lengths)
    inputs = pair[0].astype(jnp.float32).reshape(total, own, P_SIZE)
    cot = pair[1].astype(jnp.float32).reshape(total, own, P_SIZE)

    def whole_of(i, brow, crow, d):
        return mixer_whole(i, brow, crow, d, gains, segment)

    mixed, pull = jax.vjp(
        whole_of, inputs, b_all.astype(jnp.float32), c_all.astype(jnp.float32), decay
    )
    grad_x, grad_b, grad_c, grad_decay = pull(cot)
    back = jnp.stack(
        [
            mixed.reshape(total, own * P_SIZE).astype(jnp.bfloat16),
            grad_x.reshape(total, own * P_SIZE).astype(jnp.bfloat16),
        ]
    )
    back = lax.all_to_all(back, "seq", split_axis=1, concat_axis=2, tiled=True)
    grad_decay = lax.all_to_all(grad_decay, "seq", split_axis=1, concat_axis=0, tiled=True)
    return (back[0], back[1], jnp.concatenate([grad_b, grad_c], axis=1), grad_decay)


def mamba_by_stretch(
    x_input, b_rows, c_rows, decay_log, skip_gain, doc_lengths, mixer_cot, segment, offset
):
    tokens = x_input.shape[0]
    previous = doc_index(jnp.reshape(offset - 1, (1,)), doc_lengths)[0]
    before = jnp.where(offset > 0, previous, -1)
    heads_here = skip_gain.shape[0]
    inputs = x_input.astype(jnp.float32).reshape(tokens, heads_here, P_SIZE)
    b_float = b_rows.astype(jnp.float32)
    c_float = c_rows.astype(jnp.float32)
    cot_float = mixer_cot.astype(jnp.float32).reshape(tokens, heads_here, P_SIZE)

    def stretch_of(inp, brow, crow, decay, state_in):
        return mixer_stretch(inp, brow, crow, decay, skip_gain, segment, before, state_in)

    cumulated = cumulate(decay_log)
    factor = carry_factor(cumulated, segment, before)
    summary = local_state(inputs, b_float, cumulated, segment)
    zero_state = jnp.zeros_like(summary)
    identity = (jnp.ones_like(factor), zero_state)
    state_in = entering_2((factor, summary), "seq", combine_states, identity, False)[1]
    (mixed, state_out), pull = jax.vjp(stretch_of, inputs, b_float, c_float, decay_log, state_in)
    adjoint_local = pull((cot_float, zero_state))[4]
    adjoint_out = entering_2((factor, adjoint_local), "seq", combine_states, identity, True)[1]
    grad_x, grad_b, grad_c, grad_decay, unused = pull((cot_float, adjoint_out))
    head_count = lax.axis_size("head")
    if head_count == 2:
        other_b, other_c = lax.ppermute((grad_b, grad_c), "head", [(0, 1), (1, 0)])
        grad_b, grad_c = (grad_b + other_b, grad_c + other_c)
    else:
        grad_b, grad_c = lax.psum((grad_b, grad_c), "head")
    mixer_out = mixed.reshape(tokens, heads_here * P_SIZE).astype(jnp.bfloat16)
    x_grad = grad_x.reshape(tokens, heads_here * P_SIZE).astype(jnp.bfloat16)
    return (mixer_out, x_grad, grad_b, grad_c, grad_decay)


def on_device(
    x_input,
    b_rows,
    c_rows,
    decay_log,
    skip_gain,
    doc_lengths,
    queries,
    attention_key_rows,
    values,
    mixer_cot,
    attention_output_cotangent,
):
    tokens = x_input.shape[0]
    offset = lax.axis_index("seq") * tokens
    total_len = tokens * lax.axis_size("seq")
    positions = offset + jnp.arange(tokens, dtype=jnp.int32)
    segment = doc_index(positions, doc_lengths)
    heads_here = skip_gain.shape[0]
    by_heads = heads_here % lax.axis_size("seq") == 0
    key_width = attention_key_rows.shape[1]
    state_width = b_rows.shape[1]
    pieces = [attention_key_rows, values] + ([b_rows, c_rows] if by_heads else [])
    gathered = lax.all_gather(jnp.concatenate(pieces, axis=1), "seq", axis=0, tiled=True)
    key_all, value_all = (gathered[:, :key_width], gathered[:, key_width : 2 * key_width])
    if by_heads:
        b_all = gathered[:, 2 * key_width : 2 * key_width + state_width]
        c_all = gathered[:, 2 * key_width + state_width :]
        mixer_out, x_grad, bc_part, grad_decay = mamba_by_heads(
            x_input, b_all, c_all, decay_log, skip_gain, doc_lengths, mixer_cot
        )
    else:
        mixer_out, x_grad, grad_b, grad_c, grad_decay = mamba_by_stretch(
            x_input, b_rows, c_rows, decay_log, skip_gain, doc_lengths, mixer_cot, segment, offset
        )
    logit_scale = 1.0 / math.sqrt(HEAD_SIZE)
    groups = attention_key_rows.shape[1] // HEAD_SIZE
    heads_per_group = queries.shape[1] // HEAD_SIZE // groups
    key_span = min(512, total_len)
    blocks = total_len // key_span
    last_pos = offset + tokens - 1
    query_grid = queries.reshape(tokens, groups, heads_per_group, HEAD_SIZE)
    cotangent_table = attention_output_cotangent.reshape(tokens, groups, heads_per_group, HEAD_SIZE)

    def block_view(number):
        anchor = number * key_span
        key_blk = lax.dynamic_slice_in_dim(key_all, anchor, key_span, 0).reshape(
            key_span, groups, HEAD_SIZE
        )
        value_blk = lax.dynamic_slice_in_dim(value_all, anchor, key_span, 0).reshape(
            key_span, groups, HEAD_SIZE
        )
        key_pos = anchor + jnp.arange(key_span, dtype=jnp.int32)
        allowed = (key_pos[None, :] <= positions[:, None]) & (
            doc_index(key_pos, doc_lengths)[None, :] == segment[:, None]
        )
        scores = (
            jnp.einsum("tgrd,kgd->grtk", query_grid, key_blk, preferred_element_type=jnp.float32)
            * logit_scale
        )
        scores = jnp.where(allowed[None, None], scores, big_negative)
        return (anchor, key_blk, value_blk, allowed, scores)

    def visit(number, carried, work):
        return lax.cond(
            number * key_span <= last_pos,
            lambda inner: work(number, inner),
            lambda inner: inner,
            carried,
        )

    def stats_step(number, carried):
        row_peak, row_total = carried
        anchor, key_blk, value_blk, allowed, scores = block_view(number)
        new_peak = jnp.maximum(row_peak, jnp.max(scores, axis=-1))
        fresh = jnp.sum(
            jnp.where(allowed[None, None], jnp.exp(scores - new_peak[..., None]), 0.0), axis=-1
        )
        return (new_peak, row_total * jnp.exp(row_peak - new_peak) + fresh)

    stat_shape = (groups, heads_per_group, tokens)
    row_peak, row_total = lax.fori_loop(
        0,
        blocks,
        lambda number, carried: visit(number, carried, stats_step),
        (jnp.full(stat_shape, big_negative, jnp.float32), jnp.zeros(stat_shape, jnp.float32)),
    )
    log_norm = row_peak + jnp.log(row_total)

    def output_step(number, totals):
        anchor, key_blk, value_blk, allowed, scores = block_view(number)
        weights = jnp.where(allowed[None, None], jnp.exp(scores - log_norm[..., None]), 0.0).astype(
            jnp.bfloat16
        )
        return totals + jnp.einsum(
            "grtk,kgd->tgrd", weights, value_blk, preferred_element_type=jnp.float32
        )

    attention_table = lax.fori_loop(
        0,
        blocks,
        lambda number, carried: visit(number, carried, output_step),
        jnp.zeros((tokens, groups, heads_per_group, HEAD_SIZE), jnp.float32),
    ).astype(jnp.bfloat16)
    row_products = jnp.einsum(
        "bkfh,bkfh->kfb", cotangent_table, attention_table, preferred_element_type=jnp.float32
    )

    def grad_terms(allowed, scores, value_blk):
        probs_full = jnp.where(allowed[None, None], jnp.exp(scores - log_norm[..., None]), 0.0)
        grad_prob = jnp.einsum(
            "tgrd,kgd->grtk", cotangent_table, value_blk, preferred_element_type=jnp.float32
        )
        grad_score = (probs_full * (grad_prob - row_products[..., None])).astype(jnp.bfloat16)
        return (probs_full.astype(jnp.bfloat16), grad_score)

    query_zero = jnp.zeros((tokens, groups, heads_per_group, HEAD_SIZE), jnp.float32)

    def full_step(number, carried):
        grad_query, term_key, term_value = carried
        anchor, key_blk, value_blk, allowed, scores = block_view(number)
        weights, grad_score = grad_terms(allowed, scores, value_blk)
        grad_query = grad_query + jnp.einsum(
            "grtk,kgd->tgrd", grad_score, key_blk, preferred_element_type=jnp.float32
        )
        key_part = jnp.einsum(
            "grtk,tgrd->kgd", grad_score, query_grid, preferred_element_type=jnp.float32
        ).reshape(key_span, groups * HEAD_SIZE)
        value_part = jnp.einsum(
            "grtk,tgrd->kgd", weights, cotangent_table, preferred_element_type=jnp.float32
        ).reshape(key_span, groups * HEAD_SIZE)
        term_key = lax.dynamic_update_slice_in_dim(term_key, key_part, anchor, 0)
        term_value = lax.dynamic_update_slice_in_dim(term_value, value_part, anchor, 0)
        return (grad_query, term_key, term_value)

    term_zero = jnp.zeros((total_len, groups * HEAD_SIZE), jnp.float32)
    grad_query, term_key, term_value = lax.fori_loop(
        0,
        blocks,
        lambda number, carried: visit(number, carried, full_step),
        (query_zero, term_zero, term_zero),
    )
    sums = [term_key, term_value] + ([bc_part] if by_heads else [])
    kv_total = lax.psum_scatter(
        jnp.concatenate(sums, axis=1), "seq", scatter_dimension=0, tiled=True
    )
    key_gradient_total = kv_total[:, : groups * HEAD_SIZE]
    value_gradient_total = kv_total[:, groups * HEAD_SIZE : 2 * groups * HEAD_SIZE]
    if by_heads:
        bc_sum = kv_total[:, 2 * groups * HEAD_SIZE :]
        if lax.axis_size("head") == 2:
            bc_sum = bc_sum + lax.ppermute(bc_sum, "head", [(0, 1), (1, 0)])
        else:
            bc_sum = lax.psum(bc_sum, "head")
        grad_b, grad_c = (bc_sum[:, :state_width], bc_sum[:, state_width:])
    attn_out = attention_table.reshape(tokens, groups * heads_per_group * HEAD_SIZE)
    q_grad = (
        (grad_query * logit_scale)
        .reshape(tokens, groups * heads_per_group * HEAD_SIZE)
        .astype(jnp.bfloat16)
    )
    key_gradient = (key_gradient_total * logit_scale).astype(jnp.bfloat16)
    value_gradient = value_gradient_total.astype(jnp.bfloat16)
    return (
        mixer_out,
        attn_out,
        x_grad,
        grad_b,
        grad_c,
        grad_decay,
        q_grad,
        key_gradient,
        value_gradient,
    )


def solution(mesh):
    placed = (
        P(("groups", "seq"), "head"),
        P(("groups", "seq"), None),
        P(("groups", "seq"), None),
        P(("groups", "head"), "seq"),
        P("head"),
        P("groups"),
        P(("groups", "seq"), "head"),
        P(("groups", "seq"), "head"),
        P(("groups", "seq"), "head"),
        P(("groups", "seq"), "head"),
        P(("groups", "seq"), "head"),
    )
    return jax.shard_map(
        on_device,
        mesh=mesh,
        in_specs=placed,
        out_specs=(
            P(("groups", "seq"), "head"),
            P(("groups", "seq"), "head"),
            P(("groups", "seq"), "head"),
            P(("groups", "seq"), None),
            P(("groups", "seq"), None),
            P(("groups", "head"), "seq"),
            P(("groups", "seq"), "head"),
            P(("groups", "seq"), "head"),
            P(("groups", "seq"), "head"),
        ),
        check_vma=False,
    )
```

profile of v0, /device:TPU:1, one launch (start us, length us, event | category | flops | bytes accessed | tf_op | source)
XLA Modules:
  0.0 266.9 jit_solution(8798041764163728764)
XLA Ops:
  11.6 6.4 %all-to-all-start.1 = ((f32[8,2,128]{2,1,0:T(2,128)}), f32[8,2,128]{2,1,0:T(2,128)S(1)}, u32[]{:S(2)}, u32[]{:S(2)}) async-start(f32[8,2,128]{2,1,0:T(2,128)} %bitcast.332), calls=%async_computation.1 | async-start | bytes 16384 | tf_op jit(solution)/shard_map/all_to_all | solution.py:115
  20.2 2.0 copy.341
  23.4 4.3 %all-to-all-start = ((bf16[2,128,2048]{1,0,2:T(2,128)(2,1)}), bf16[2,128,2048]{1,0,2:T(2,128)(2,1)S(1)}, u32[]{:S(2)}, u32[]{:S(2)}) async-start(bf16[2,128,2048]{1,0,2:T(2,128)(2,1)} %copy.341), calls=%async_computation | async-start | bytes 2097152 | tf_op jit(solution)/shard_map/all_to_all | solution.py:112
  33.2 34.0 %all-to-all-done = bf16[2,128,2048]{1,0,2:T(2,128)(2,1)S(1)} async-done(((bf16[2,128,2048]{1,0,2:T(2,128)(2,1)}), bf16[2,128,2048]{1,0,2:T(2,128)(2,1)S(1)}, u32[]{:S(2)}, u32[]{:S(2)}) %all-to-all-start) | async-done | bytes 1048608 | tf_op jit(solution)/shard_map/all_to_all | solution.py:112
  67.5 2.4 all-gather.2.cloned.1.call-done
  72.5 2.3 fusion.35
  74.9 23.3 %while.88 = (s32[]{:T(128)}, f32[2,128,128]{2,1,0:T(8,128)S(1)}, f32[8,2,128,128]{3,2,1,0:T(8,128)S(1)}, f32[8,2,1,1]{1,3,2,0:T(1,128)}, f32[8,2]{1,0:T(8,128)},...) while((s32[]{:T(128)}, f32[2,128,128]{2,1,0:T(8,128)S(1)}, ...), condition=%wide.region_4.5_spmd.clone, body=%wide.region_3.4_spmd.clone.sunk | while | flops 131075 | bytes 656528 | solution.py:96
  99.5 2.9 %fusion.52 = (f32[8,128,2]{1,2,0:T(2,128)S(1)}, f32[8,128,256]{1,2,0}) fusion(bf16[8,128,2,128]{1,3,2,0:T(8,128)(2,1)S(1)} %bitcast.283, bf16[8,128,128]{2,1,0:T(8,128)(2,1)S(1)} %bitcast.294, f32[8,128,256]{1,2,0:T(8,128)} %bitcast.306), kind=kOutput, calls=%fused_computation.87 | convolution fusion | flops 403437568 | bytes 2891776
  104.0 2.7 %fusion.51 = f32[8,128,128]{2,1,0:T(8,128)} fusion(f32[8,2,128,128]{3,2,1,0:T(8,128)S(1)} %get-tuple-element.1737, bf16[8,128,2,128]{1,3,2,0:T(8,128)(2,1)S(1)} %bitcast.285, f32[8,128,2]{1,2,0:T(2,128)S(1)} %copy.352), kind=kOutput, calls=%fused_computation.84 | convolution fusion | flops 403177472 | bytes 2105344 | tf_op jit(solution)/shard_map/transpose(jvp(vmap(tn,hnp->thp)))/dot_general | solution.py:66
  108.5 14.9 %while.89 = (s32[]{:T(128)}, f32[2,128,128]{2,1,0:T(8,128)S(1)}, f32[8,2]{1,0:T(8,128)S(1)}, f32[8,2,128,128]{3,2,1,0:T(8,128)S(1)}, f32[8,2,128,128]{2,3,1,0:T(...) while((s32[]{:T(128)}, f32[2,128,128]{2,1,0:T(8,128)S(1)}, ...), condition=%wide.region_7.8_spmd.clone, body=%wide.region_5.7_spmd.clone.sunk | while | flops 196610 | bytes 1310920 | solution.py:96
  127.4 3.3 %while.86 = (s32[]{:T(128)}, f32[128,2,4,128]{0,3,2,1:T(8,128)}, s32[]{:T(128)}, bf16[1024,256]{0,1:T(8,128)(2,1)S(1)}, s32[4]{0:T(128)S(1)}, /*index=5*/s32[128...) while((s32[]{:T(128)}, f32[128,2,4,128]{0,3,2,1:T(8,128)}, ...), condition=%wide.region_22.23_spmd.clone, body=%wide.region_17.22_spmd.clone.sunk | while | flops 271390848 | bytes 3031901 | solution.py:273
  127.4 3.3 %conditional.10 = (f32[128,2,4,128]{0,3,2,1:T(8,128)}) conditional(s32[]{:T(128)} %convert_element_type.165, f32[128,2,4,128]{0,3,2,1:T(8,128)} %get-tuple-element.1807, (s32[]{:T(128)}, bf16[1024,256]{0,1:T(8,128)(2,1)S(1)}, s32[]{:T(128)}, s32[4]{0:T(128)S(1)}, s32[128]{0:T(128)S(1)}, /*index=5*/bf16[1024,256]{0,1:T(8,128)(2,1)S(1)}, ...), branch_computations={%region_18.18_spmd, %region_19.21_spmd} | conditional | flops 271390848 | bytes 3031158 | solution.py:239
  128.0 2.8 %fusion.13 = f32[128,2,4,128]{0,3,2,1:T(8,128)} fusion(f32[128,2,4,128]{0,3,2,1:T(8,128)} %get-tuple-element.792, bf16[512,2,128,1]{0,2,3,1:T(8,128)(2,1)S(1)} %bitcast.298, bf16[512,2,128,1]{0,2,3,1:T(8,128)(2,1)S(1)} %bitcast.297, bf16[128,2,4,128]{3,0,2,1:T(8,128)(2,1)S(1)} %get-tuple-element.799, f32[2,4,128]{2,1,0:T(4,128)S(1)} %get-tuple-element.800, ...), kind=kOutput, calls=%fused_computation.19 | convolution fusion | flops 271187968 | bytes 1904640 | tf_op jit(solution)/shard_map/while/body/eval_jaxpr/cond/branch_1_fun/grtk,kgd->tgrd/dot_general | solution.py:269
  130.7 3.5 %fusion.53 = (f32[8,128,128]{1,2,0:T(8,128)}, f32[8,2,128,128]{3,2,1,0:T(8,128)}) fusion(f32[8,128,2]{1,2,0:T(2,128)S(1)} %copy.353, f32[8,2,128,128]{3,2,1,0:T(8,128)S(1)} %get-tuple-element.864, bf16[8,128,2,128]{1,3,2,0:T(8,128)(2,1)} %bitcast.301), kind=kOutput, calls=%fused_computation.91 | convolution fusion | flops 403046400 | bytes 3153920 | tf_op jit(solution)/shard_map/transpose(jvp(vmap(hs,sn,shp->hnp)))/dot_general | solution.py:50
  134.3 2.1 copy.423
  136.4 2.5 convolution_add_fusion
  140.4 1.8 fusion.60
  144.5 5.8 %while.87 = (s32[]{:T(128)}, f32[128,2,4,128]{0,3,2,1:T(8,128)S(1)}, f32[1024,256]{0,1:T(8,128)}, f32[1024,256]{0,1:T(8,128)}, s32[]{:T(128)}, /*index=5*/bf16[1...) while((s32[]{:T(128)}, ...), condition=%wide.region_28.29_spmd.clone, body=%wide.region_23.28_spmd.clone.sunk | while | flops 675616896 | bytes 33444932 | solution.py:311
  144.5 5.8 %conditional.11 = ((f32[128,2,4,128]{0,3,2,1:T(8,128)S(1)}, f32[1024,256]{0,1:T(8,128)}, f32[1024,256]{0,1:T(8,128)})) conditional(s32[]{:T(128)} %convert_element_type.166, (f32[128,2,4,128]{0,3,2,1:T(8,128)S(1)}, f32[1024,256]{0,1:T(8,128)}, f32[1024,256]{0,1:T(8,128)}) %tuple.226, (s32[]{:T(128)}, bf16[1024,256]{0,1:T(8,128)(2,1)S(1)}, ...), branch_computations={%region_24.24_spmd, %region_25.27_spmd} | conditional | flops 675616896 | bytes 33444102 | solution.py:239
  150.3 2.7 %copy.377 = f32[1024,256]{1,0:T(8,128)} copy(f32[1024,256]{0,1:T(8,128)} %get-tuple-element.869) | data formatting | bytes 2097152 | tf_op jit(solution)/shard_map/while | solution.py:311
  154.3 3.6 %pad_maximum_fusion = f32[1024,768]{1,0:T(8,128)} fusion(f32[1024,128]{1,0:T(8,128)S(1)} %bitcast.307, f32[1024,128]{1,0:T(8,128)} %bitcast.308, f32[1024,256]{1,0:T(8,128)} %copy.377, f32[1024,256]{1,0:T(8,128)} %copy.376), kind=kLoop, calls=%fused_computation.65 | loop fusion | flops 2359296 | bytes 6291456 | tf_op jit(solution)/shard_map/concatenate | solution.py:319
  159.8 2.1 fusion.43
  161.9 2.3 fusion.47
  164.9 3.0 %fusion.46 = bf16[8,128,2,128]{1,3,2,0:T(8,128)(2,1)S(1)} fusion(bf16[8,128,2,128]{1,3,2,0:T(8,128)(2,1)S(1)} %bitcast.302, f32[8,128,2,128]{1,3,2,0:T(8,128)} %bitcast.314, f32[2]{0:T(128)S(1)} %dynamic_slice.54, f32[8,128,2]{1,2,0:T(2,128)S(1)} %copy.352, f32[8,128,128]{2,1,0:T(8,128)} %fusion.90, f32[8,2,128]{2,1,0:T(2,128)S(1)} %copy-done.36, ...), kind=kOutput, calls=%fused_computation.81 | convolution fusion | flops 405012480 | bytes 2768904 | tf_op jit(solution)/shard_map/jvp(vmap(hts,shp->thp))/dot_general | solution.py:64
  169.8 2.5 reduce_window_sum.46
  172.4 2.5 reduce_window_sum.47
  175.5 13.2 %all-to-all-start.3 = ((f32[2,8,128]{2,0,1:T(2,128)}), f32[2,8,128]{2,0,1:T(2,128)S(1)}, u32[]{:S(2)}, u32[]{:S(2)}) async-start(f32[2,8,128]{2,0,1:T(2,128)} %copy.384), calls=%async_computation.4 | async-start | bytes 16384 | tf_op jit(solution)/shard_map/all_to_all | solution.py:135
  188.8 2.1 copy.362
  190.9 3.4 %all-to-all-done.3 = f32[2,8,128]{2,0,1:T(2,128)S(1)} async-done(((f32[2,8,128]{2,0,1:T(2,128)}), f32[2,8,128]{2,0,1:T(2,128)S(1)}, u32[]{:S(2)}, u32[]{:S(2)}) %all-to-all-start.3) | async-done | bytes 8224 | tf_op jit(solution)/shard_map/all_to_all | solution.py:135
  194.3 3.6 %all-to-all-start.2 = ((bf16[2,1024,256]{2,0,1:T(2,128)(2,1)}), bf16[2,1024,256]{2,0,1:T(2,128)(2,1)S(1)}, u32[]{:S(2)}, u32[]{:S(2)}) async-start(bf16[2,1024,256]{2,0,1:T(2,128)(2,1)} %copy.362), calls=%async_computation.2 | async-start | bytes 2097152 | tf_op jit(solution)/shard_map/all_to_all | solution.py:134
  199.7 25.4 %all-to-all-done.2 = bf16[2,1024,256]{2,0,1:T(2,128)(2,1)S(1)} async-done(((bf16[2,1024,256]{2,0,1:T(2,128)(2,1)}), bf16[2,1024,256]{2,0,1:T(2,128)(2,1)S(1)}, u32[]{:S(2)}, u32[]{:S(2)}) %all-to-all-start.2) | async-done | bytes 1048608 | tf_op jit(solution)/shard_map/all_to_all | solution.py:134
  225.2 27.3 %reduce-scatter.2.cloned.1.call-done = f32[128,768]{1,0:T(8,128)} async-done(((f32[1024,768]{1,0:T(8,128)}), f32[128,768]{1,0:T(8,128)}) %reduce-scatter.2.cloned.1.call-update) | async-done | bytes 393232 | tf_op jit(solution)/shard_map/reduce_scatter | solution.py:318
  (296 shorter events, 91.7 us)
Async XLA Ops:
  7.2 62.7 %all-gather.2.cloned.1.call-start = ((), (), s32[]{:S(2)}) async-start(), calls=%async_computation.5 | async-start | bytes 1769472 | tf_op jit(solution)/shard_map/all_gather | solution.py:198
  11.6 11.8 %all-to-all-start.1 = ((f32[8,2,128]{2,1,0:T(2,128)}), f32[8,2,128]{2,1,0:T(2,128)S(1)}, u32[]{:S(2)}, u32[]{:S(2)}) async-start(f32[8,2,128]{2,1,0:T(2,128)} %bitcast.332), calls=%async_computation.1 | async-start | bytes 16384 | tf_op jit(solution)/shard_map/all_to_all | solution.py:115
  20.2 7.6 %copy-start.26 = (bf16[128,1024]{1,0:T(8,128)(2,1)S(1)}, bf16[128,1024]{1,0:T(8,128)(2,1)}, u32[]{:S(2)}) copy-start(bf16[128,1024]{1,0:T(8,128)(2,1)} %param.37) | copy-start | bytes 786436
  20.2 7.7 %copy-start.27 = (bf16[128,1024]{1,0:T(8,128)(2,1)S(1)}, bf16[128,1024]{1,0:T(8,128)(2,1)}, u32[]{:S(2)}) copy-start(bf16[128,1024]{1,0:T(8,128)(2,1)} %param.33) | copy-start | bytes 786436
  23.4 43.8 %all-to-all-start = ((bf16[2,128,2048]{1,0,2:T(2,128)(2,1)}), bf16[2,128,2048]{1,0,2:T(2,128)(2,1)S(1)}, u32[]{:S(2)}, u32[]{:S(2)}) async-start(bf16[2,128,2048]{1,0,2:T(2,128)(2,1)} %copy.341), calls=%async_computation | async-start | bytes 2097152 | tf_op jit(solution)/shard_map/all_to_all | solution.py:112
  27.7 224.8 %reduce-scatter.2.cloned.1.call-start = ((), (), s32[]{:S(2)}) async-start(), calls=%async_computation.6 | async-start | bytes 3538944 | tf_op jit(solution)/shard_map/reduce_scatter | solution.py:318
  29.6 37.8 %copy-start.37 = (f32[8]{0:T(128)}, f32[8]{0:T(128)S(1)}, u32[]{:S(2)}) copy-start(f32[8]{0:T(128)S(1)} %convert_reduce_fusion.4) | copy-start | bytes 100
  30.9 36.5 %copy-start.31 = (f32[8,128]{1,0:T(8,128)}, f32[8,128]{1,0:T(8,128)S(1)}, u32[]{:S(2)}) copy-start(f32[8,128]{1,0:T(8,128)S(1)} %get-tuple-element.1394) | copy-start | bytes 12292
  31.1 71.3 %copy-start.28 = (pred[8,128,128]{2,1,0:T(8,128)(4,1)}, pred[8,128,128]{2,1,0:T(8,128)(4,1)S(1)}, u32[]{:S(2)}) copy-start(pred[8,128,128]{2,1,0:T(8,128)(4,1)S(1)} %compare_and_fusion.3) | copy-start | bytes 393220
  32.5 35.0 %copy-start.34 = (f32[8,2]{0,1:T(2,128)}, f32[8,2]{0,1:T(2,128)S(1)}, u32[]{:S(2)}) copy-start(f32[8,2]{0,1:T(2,128)S(1)} %slice_reduce_fusion) | copy-start | bytes 196
  67.5 34.9 %copy-start.10 = (bf16[1,8,128,256]{2,3,1,0:T(8,128)(2,1)}, bf16[1,8,128,256]{2,3,1,0:T(8,128)(2,1)S(1)}, u32[]{:S(2)}) copy-start(bf16[1,8,128,256]{2,3,1,0:T(8,128)(2,1)S(1)} %get-tuple-element.1386) | copy-start | bytes 1572868
  67.5 39.2 %copy-start.1 = (bf16[1,8,128,256]{2,3,1,0:T(8,128)(2,1)}, bf16[1,8,128,256]{2,3,1,0:T(8,128)(2,1)S(1)}, u32[]{:S(2)}) copy-start(bf16[1,8,128,256]{2,3,1,0:T(8,128)(2,1)S(1)} %get-tuple-element.1387) | copy-start | bytes 1572868
  71.2 35.6 %copy-start.6 = (bf16[1024,128]{1,0:T(8,128)(2,1)}, bf16[1024,128]{1,0:T(8,128)(2,1)S(1)}, u32[]{:S(2)}) copy-start(bf16[1024,128]{1,0:T(8,128)(2,1)S(1)} %copy.350) | copy-start | bytes 786436
  71.3 3.5 %copy-start.3 = (bf16[1024,128]{1,0:T(8,128)(2,1)}, bf16[1024,128]{1,0:T(8,128)(2,1)S(1)}, u32[]{:S(2)}) copy-start(bf16[1024,128]{1,0:T(8,128)(2,1)S(1)} %copy.351) | copy-start | bytes 786436
  98.2 4.3 %copy-start.36 = (f32[8,2,128]{2,1,0:T(2,128)S(1)}, f32[8,2,128]{2,1,0:T(2,128)}, u32[]{:S(2)}) copy-start(f32[8,2,128]{2,1,0:T(2,128)} %copy.344) | copy-start | bytes 24580
  99.5 3.0 %copy-start.25 = (f32[8,128,128]{2,1,0:T(8,128)S(1)}, f32[8,128,128]{2,1,0:T(8,128)}, u32[]{:S(2)}) copy-start(f32[8,128,128]{2,1,0:T(8,128)} %fusion.90) | copy-start | bytes 1572868
  130.7 5.6 %copy-start.4 = (bf16[1024,128]{1,0:T(8,128)(2,1)S(1)}, bf16[1024,128]{1,0:T(8,128)(2,1)}, u32[]{:S(2)}) copy-start(bf16[1024,128]{1,0:T(8,128)(2,1)} %copy-done.3) | copy-start | bytes 786436
  134.3 4.6 %copy-start.7 = (bf16[1024,128]{1,0:T(8,128)(2,1)S(1)}, bf16[1024,128]{1,0:T(8,128)(2,1)}, u32[]{:S(2)}) copy-start(bf16[1024,128]{1,0:T(8,128)(2,1)} %copy-done.6) | copy-start | bytes 786436
  150.2 2.7 %copy-start.15 = (f32[1024,256]{0,1:T(8,128)S(1)}, f32[1024,256]{0,1:T(8,128)}, u32[]{:S(2)}) copy-start(f32[1024,256]{0,1:T(8,128)} %get-tuple-element.868) | copy-start | bytes 3145732
  150.2 4.0 %copy-start.19 = (f32[8,128,128]{2,1,0:T(8,128)S(1)}, f32[8,128,128]{2,1,0:T(8,128)}, u32[]{:S(2)}) copy-start(f32[8,128,128]{2,1,0:T(8,128)} %convolution_add_fusion) | copy-start | bytes 1572868
  157.9 4.0 %copy-start.9 = (f32[8,128,128]{2,1,0:T(8,128)S(1)}, f32[8,128,128]{2,1,0:T(8,128)}, u32[]{:S(2)}) copy-start(f32[8,128,128]{2,1,0:T(8,128)} %copy-done.8) | copy-start | bytes 1572868
  161.9 2.9 %copy-start.11 = (bf16[1,8,128,256]{2,3,1,0:T(8,128)(2,1)S(1)}, bf16[1,8,128,256]{2,3,1,0:T(8,128)(2,1)}, u32[]{:S(2)}) copy-start(bf16[1,8,128,256]{2,3,1,0:T(8,128)(2,1)} %copy-done.10) | copy-start | bytes 1572868
  164.8 4.5 %copy-start.35 = (f32[8,2]{0,1:T(2,128)S(1)}, f32[8,2]{0,1:T(2,128)}, u32[]{:S(2)}) copy-start(f32[8,2]{0,1:T(2,128)} %copy-done.34) | copy-start | bytes 196
  164.8 4.5 %copy-start.38 = (f32[8]{0:T(128)S(1)}, f32[8]{0:T(128)}, u32[]{:S(2)}) copy-start(f32[8]{0:T(128)} %copy-done.37) | copy-start | bytes 100
  164.9 4.6 %copy-start.12 = (f32[8,2,128,128]{3,2,1,0:T(8,128)S(1)}, f32[8,2,128,128]{3,2,1,0:T(8,128)}, u32[]{:S(2)}) copy-start(f32[8,2,128,128]{3,2,1,0:T(8,128)} %get-tuple-element.1401) | copy-start | bytes 3145732
  164.9 4.6 %copy-start.20 = (f32[8,128,128]{1,2,0:T(8,128)S(1)}, f32[8,128,128]{1,2,0:T(8,128)}, u32[]{:S(2)}) copy-start(f32[8,128,128]{1,2,0:T(8,128)} %copy.446) | copy-start | bytes 1572868
  169.2 19.5 %copy-start.22 = (bf16[1,1024,256]{1,2,0:T(8,128)(2,1)S(1)}, bf16[1,1024,256]{1,2,0:T(8,128)(2,1)}, u32[]{:S(2)}) copy-start(bf16[1,1024,256]{1,2,0:T(8,128)(2,1)} %convert_element_type.115) | copy-start | bytes 1572868
  175.5 18.8 %all-to-all-start.3 = ((f32[2,8,128]{2,0,1:T(2,128)}), f32[2,8,128]{2,0,1:T(2,128)S(1)}, u32[]{:S(2)}, u32[]{:S(2)}) async-start(f32[2,8,128]{2,0,1:T(2,128)} %copy.384), calls=%async_computation.4 | async-start | bytes 16384 | tf_op jit(solution)/shard_map/all_to_all | solution.py:135
  188.8 9.1 %copy-start.23 = (bf16[128,2,4,128]{0,3,2,1:T(8,128)(2,1)S(1)}, bf16[128,2,4,128]{0,3,2,1:T(8,128)(2,1)}, u32[]{:S(2)}) copy-start(bf16[128,2,4,128]{0,3,2,1:T(8,128)(2,1)} %get-tuple-element.1371) | copy-start | bytes 786436
  194.3 30.7 %all-to-all-start.2 = ((bf16[2,1024,256]{2,0,1:T(2,128)(2,1)}), bf16[2,1024,256]{2,0,1:T(2,128)(2,1)S(1)}, u32[]{:S(2)}, u32[]{:S(2)}) async-start(bf16[2,1024,256]{2,0,1:T(2,128)(2,1)} %copy.362), calls=%async_computation.2 | async-start | bytes 2097152 | tf_op jit(solution)/shard_map/all_to_all | solution.py:134
  253.4 4.7 %collective-permute-start = (f32[128,256]{1,0:T(8,128)S(1)}, f32[128,256]{1,0:T(8,128)S(1)}, u32[]{:S(2)}, u32[]{:S(2)}) collective-permute-start(f32[128,256]{1,0:T(8,128)S(1)} %slice.80), channel_id=1, source_target_pairs={{0,1},{1,0},{2,3},{3,2},{4,5},{5,4},{6,7},{7,6},{8,9},{9,8},{10,11... | collective-permute-start | bytes 393224 | tf_op jit(solution)/shard_map/ppermute | solution.py:326
  254.9 2.6 copy-start.24
  (16 other events, 23.8 us)
Sparse Core Ops, SparseCore 0:
  11.7 58.1 all-gather.1
  158.0 94.3 reduce-scatter.1
where the time goes:
time: 269 us; the launch traced here: 267 us
  waiting for transfers between devices  93.6 us (35%)
  local copies, waits for them, and re-layouts  68.2 us (25%)
  matrix products  32.8 us (12%)
  starting transfers between devices  29 us (11%)
  other arithmetic  28 us (10%)
  between operations  14.7 us (5%)
    all_to_all x1, waiting for transfers between devices, mamba_by_heads(): lax.all_to_all(jnp.stack([x_input, mixer_cot]), 'seq', split_axis=2, conc...  34 us
    reduce_scatter x1, waiting for transfers between devices, on_device(): lax.psum_scatter(jnp.concatenate(sums, axis=1), 'seq', scatter_dimension=...  27.3 us
    all_to_all x1, waiting for transfers between devices, mamba_by_heads(): back = lax.all_to_all(back, 'seq', split_axis=1, concat_axis=2, tiled=True)  25.4 us
    all_to_all x1, starting transfers between devices, mamba_by_heads(): lax.all_to_all(grad_decay, 'seq', split_axis=1, concat_axis=0, tiled=True)  13.2 us
    mul x16, local copies, waits for them, and re-layouts, advance(): return (fac[:, None, None] * carried + summ, carried)  10.9 us
    unnamed x86, local copies, waits for them, and re-layouts  10.1 us
    dynamic_update_slice x16, local copies, waits for them, and re-layouts, mixer_whole(): lax.scan(advance, jnp.zeros_like(summary[0]), (factor, summary))  9.87 us
    dot_general x3, matrix products, local_state(): jnp.einsum('hs,sn,shp->hnp', weights, b_float, inputs, precision=precise)  8.09 us
  transfers between devices with their start and end apart: 7, of which 6 were waited for; matrix products, arithmetic and copies ran while one was open for 13% of the time, Pallas kernels for 0%

commit v1 on v0

--- a/solution.py
+++ b/solution.py
@@ -9,6 +9,12 @@
 TOK_SPAN = 128
 precise = lax.Precision.HIGHEST
 big_negative = -1e30
+
+
+def form_ticks(content):
+    return jnp.concatenate(
+        lax.all_to_all(jnp.stack(jnp.split(content, lax.axis_size("seq"), 0), 0), "seq", 0, 0), 1
+    )
 
 
 def entering_2(part, axis, combine, identity, reverse):
@@ -112,7 +118,7 @@
     pair = lax.all_to_all(
         jnp.stack([x_input, mixer_cot]), "seq", split_axis=2, concat_axis=1, tiled=True
     )
-    decay = lax.all_to_all(decay_log, "seq", split_axis=0, concat_axis=1, tiled=True)
+    decay = form_ticks(decay_log)
     gains = lax.dynamic_slice_in_dim(skip_gain, place * own, own)
     segment = doc_index(jnp.arange(total, dtype=jnp.int32), doc_lengths)
     inputs = pair[0].astype(jnp.float32).reshape(total, own, P_SIZE)

time: 269 us -> 272 us (1.011)
  local copies, waits for them, and re-layouts: 68.2 us -> 77.2 us
  waiting for transfers between devices: 93.6 us -> 86.6 us
    unnamed x86 -> x91, local copies, waits for them, and re-layouts: 10.1 us -> 18.8 us
  transfers between devices with their start and end apart: 7 -> 7, of which waited for: 6 -> 5; matrix products, arithmetic and copies ran while one was open for 13% -> 17% of each run, Pallas kernels for 0% -> 0%
where the time goes in v1:
time: 272 us; the launch traced here: 270 us
  waiting for transfers between devices  86.6 us (32%)
  local copies, waits for them, and re-layouts  77.2 us (28%)
  matrix products  32.7 us (12%)
  starting transfers between devices  29.4 us (11%)
  other arithmetic  28.8 us (11%)
  between operations  14.7 us (5%)
    all_to_all x1, waiting for transfers between devices, mamba_by_heads(): lax.all_to_all(jnp.stack([x_input, mixer_cot]), 'seq', split_axis=2, conc...  32 us
    reduce_scatter x1, waiting for transfers between devices, on_device(): lax.psum_scatter(jnp.concatenate(sums, axis=1), 'seq', scatter_dimension=...  26.3 us
    all_to_all x1, waiting for transfers between devices, mamba_by_heads(): back = lax.all_to_all(back, 'seq', split_axis=1, concat_axis=2, tiled=True)  24.8 us
    unnamed x91, local copies, waits for them, and re-layouts  18.8 us
    all_to_all x1, starting transfers between devices, mamba_by_heads(): lax.all_to_all(grad_decay, 'seq', split_axis=1, concat_axis=0, tiled=True)  13.7 us
    mul x16, local copies, waits for them, and re-layouts, advance(): return (fac[:, None, None] * carried + summ, carried)  10.9 us
    dynamic_update_slice x16, local copies, waits for them, and re-layouts, mixer_whole(): lax.scan(advance, jnp.zeros_like(summary[0]), (factor, summary))  9.87 us
    dot_general x3, matrix products, local_state(): jnp.einsum('hs,sn,shp->hnp', weights, b_float, inputs, precision=precise)  8.07 us
  transfers between devices with their start and end apart: 7, of which 5 were waited for; matrix products, arithmetic and copies ran while one was open for 17% of the time, Pallas kernels for 0%

profile of v1, /device:TPU:1, one launch (start us, length us, event | category | flops | bytes accessed | tf_op | source)
XLA Modules:
  0.0 270.0 jit_solution(10856526650221026137)
XLA Ops:
  21.6 6.4 %all-to-all-start.1 = ((f32[8,2,128]{2,1,0:T(2,128)}), f32[8,2,128]{2,1,0:T(2,128)S(1)}, u32[]{:S(2)}, u32[]{:S(2)}) async-start(f32[8,2,128]{2,1,0:T(2,128)} %constant_dynamic-update-slice_fusion.3), calls=%async_computation.1 | async-start | bytes 16384 | tf_op jit(solution)/shard_map/all_to_all | solution.py:16
  30.2 2.0 copy.341
  33.4 4.3 %all-to-all-start = ((bf16[2,128,2048]{1,0,2:T(2,128)(2,1)}), bf16[2,128,2048]{1,0,2:T(2,128)(2,1)S(1)}, u32[]{:S(2)}, u32[]{:S(2)}) async-start(bf16[2,128,2048]{1,0,2:T(2,128)(2,1)} %copy.341), calls=%async_computation | async-start | bytes 2097152 | tf_op jit(solution)/shard_map/all_to_all | solution.py:118
  43.3 32.0 %all-to-all-done = bf16[2,128,2048]{1,0,2:T(2,128)(2,1)S(1)} async-done(((bf16[2,128,2048]{1,0,2:T(2,128)(2,1)}), bf16[2,128,2048]{1,0,2:T(2,128)(2,1)S(1)}, u32[]{:S(2)}, u32[]{:S(2)}) %all-to-all-start) | async-done | bytes 1048608 | tf_op jit(solution)/shard_map/all_to_all | solution.py:118
  78.7 2.3 fusion.35
  81.1 23.3 %while.88 = (s32[]{:T(128)}, f32[2,128,128]{2,1,0:T(8,128)S(1)}, f32[8,2,128,128]{3,2,1,0:T(8,128)S(1)}, f32[8,2,1,1]{1,3,2,0:T(1,128)}, f32[8,2]{1,0:T(8,128)},...) while((s32[]{:T(128)}, f32[2,128,128]{2,1,0:T(8,128)S(1)}, ...), condition=%wide.region_4.5_spmd.clone, body=%wide.region_3.4_spmd.clone.sunk | while | flops 131075 | bytes 656528 | solution.py:102
  105.7 2.9 %fusion.52 = (f32[8,128,2]{1,2,0:T(2,128)S(1)}, f32[8,128,256]{1,2,0}) fusion(bf16[8,128,2,128]{1,3,2,0:T(8,128)(2,1)S(1)} %bitcast.298, bf16[8,128,128]{2,1,0:T(8,128)(2,1)S(1)} %bitcast.309, f32[8,128,256]{1,2,0:T(8,128)} %bitcast.321), kind=kOutput, calls=%fused_computation.87 | convolution fusion | flops 403437568 | bytes 2891776
  110.2 2.7 fusion.51
  114.6 14.9 %while.89 = (s32[]{:T(128)}, f32[2,128,128]{2,1,0:T(8,128)S(1)}, f32[8,2]{1,0:T(8,128)S(1)}, f32[8,2,128,128]{3,2,1,0:T(8,128)S(1)}, f32[8,2,128,128]{2,3,1,0:T(...) while((s32[]{:T(128)}, f32[2,128,128]{2,1,0:T(8,128)S(1)}, ...), condition=%wide.region_7.8_spmd.clone, body=%wide.region_5.7_spmd.clone.sunk | while | flops 196610 | bytes 1310920 | solution.py:102
  130.9 1.8 while.85
  133.6 3.3 %while.86 = (s32[]{:T(128)}, f32[128,2,4,128]{0,3,2,1:T(8,128)}, s32[]{:T(128)}, bf16[1024,256]{0,1:T(8,128)(2,1)S(1)}, s32[4]{0:T(128)S(1)}, /*index=5*/s32[128...) while((s32[]{:T(128)}, f32[128,2,4,128]{0,3,2,1:T(8,128)}, ...), condition=%wide.region_22.23_spmd.clone, body=%wide.region_17.22_spmd.clone.sunk | while | flops 271390848 | bytes 3031901 | solution.py:279
  133.6 3.3 %conditional.10 = (f32[128,2,4,128]{0,3,2,1:T(8,128)}) conditional(s32[]{:T(128)} %convert_element_type.165, f32[128,2,4,128]{0,3,2,1:T(8,128)} %get-tuple-element.1807, (s32[]{:T(128)}, bf16[1024,256]{0,1:T(8,128)(2,1)S(1)}, s32[]{:T(128)}, s32[4]{0:T(128)S(1)}, s32[128]{0:T(128)S(1)}, /*index=5*/bf16[1024,256]{0,1:T(8,128)(2,1)S(1)}, ...), branch_computations={%region_18.18_spmd, %region_19.21_spmd} | conditional | flops 271390848 | bytes 3031158 | solution.py:245
  134.1 2.8 %fusion.13 = f32[128,2,4,128]{0,3,2,1:T(8,128)} fusion(f32[128,2,4,128]{0,3,2,1:T(8,128)} %get-tuple-element.792, bf16[512,2,128,1]{0,2,3,1:T(8,128)(2,1)S(1)} %bitcast.313, bf16[512,2,128,1]{0,2,3,1:T(8,128)(2,1)S(1)} %bitcast.312, bf16[128,2,4,128]{3,0,2,1:T(8,128)(2,1)S(1)} %get-tuple-element.799, f32[2,4,128]{2,1,0:T(4,128)S(1)} %get-tuple-element.800, ...), kind=kOutput, calls=%fused_computation.19 | convolution fusion | flops 271187968 | bytes 1904640 | tf_op jit(solution)/shard_map/while/body/eval_jaxpr/cond/branch_1_fun/grtk,kgd->tgrd/dot_general | solution.py:275
  136.9 3.5 %fusion.53 = (f32[8,128,128]{1,2,0:T(8,128)}, f32[8,2,128,128]{3,2,1,0:T(8,128)}) fusion(f32[8,128,2]{1,2,0:T(2,128)S(1)} %copy.353, f32[8,2,128,128]{3,2,1,0:T(8,128)S(1)} %get-tuple-element.864, bf16[8,128,2,128]{1,3,2,0:T(8,128)(2,1)} %bitcast.316), kind=kOutput, calls=%fused_computation.91 | convolution fusion | flops 403046400 | bytes 3153920 | tf_op jit(solution)/shard_map/transpose(jvp(vmap(hs,sn,shp->hnp)))/dot_general | solution.py:56
  140.4 2.1 copy.423
  142.5 2.4 convolution_add_fusion
  146.4 1.8 fusion.60
  150.5 4.2 %while.87 = (s32[]{:T(128)}, f32[128,2,4,128]{0,3,2,1:T(8,128)S(1)}, f32[1024,256]{0,1:T(8,128)}, f32[1024,256]{0,1:T(8,128)}, s32[]{:T(128)}, /*index=5*/bf16[1...) while((s32[]{:T(128)}, ...), condition=%wide.region_28.29_spmd.clone, body=%wide.region_23.28_spmd.clone.sunk | while | flops 675616896 | bytes 16667605 | solution.py:317
  150.5 4.2 %conditional.11 = ((f32[128,2,4,128]{0,3,2,1:T(8,128)S(1)}, f32[1024,256]{0,1:T(8,128)}, f32[1024,256]{0,1:T(8,128)})) conditional(s32[]{:T(128)} %convert_element_type.166, (f32[128,2,4,128]{0,3,2,1:T(8,128)S(1)}, f32[1024,256]{0,1:T(8,128)}, f32[1024,256]{0,1:T(8,128)}) %tuple.226, (s32[]{:T(128)}, bf16[1024,256]{0,1:T(8,128)(2,1)S(1)}, ...), branch_computations={%region_24.24_spmd, %region_25.27_spmd} | conditional | flops 675616896 | bytes 16666774 | solution.py:245
  156.3 2.6 copy.376
  158.9 3.3 %pad_maximum_fusion = f32[1024,768]{1,0:T(8,128)} fusion(f32[1024,128]{1,0:T(8,128)S(1)} %bitcast.322, f32[1024,128]{1,0:T(8,128)} %bitcast.323, f32[1024,256]{1,0:T(8,128)S(1)} %copy.377, f32[1024,256]{1,0:T(8,128)} %copy.376), kind=kLoop, calls=%fused_computation.65 | loop fusion | flops 2359296 | bytes 6291456 | tf_op jit(solution)/shard_map/concatenate | solution.py:325
  164.1 2.1 fusion.43
  166.2 2.3 fusion.47
  169.2 3.0 %fusion.46 = bf16[8,128,2,128]{1,3,2,0:T(8,128)(2,1)S(1)} fusion(bf16[8,128,2,128]{1,3,2,0:T(8,128)(2,1)S(1)} %bitcast.317, f32[8,128,2,128]{1,3,2,0:T(8,128)} %bitcast.329, f32[2]{0:T(128)S(1)} %dynamic_slice.54, f32[8,128,2]{1,2,0:T(2,128)S(1)} %copy.352, f32[8,128,128]{2,1,0:T(8,128)} %fusion.90, f32[8,2,128]{2,1,0:T(2,128)S(1)} %copy-done.31, ...), kind=kOutput, calls=%fused_computation.81 | convolution fusion | flops 405012480 | bytes 2768904 | tf_op jit(solution)/shard_map/jvp(vmap(hts,shp->thp))/dot_general | solution.py:70
  174.1 2.5 reduce_window_sum.46
  176.7 2.5 reduce_window_sum.47
  179.8 13.7 %all-to-all-start.3 = ((f32[2,8,128]{2,0,1:T(2,128)}), f32[2,8,128]{2,0,1:T(2,128)S(1)}, u32[]{:S(2)}, u32[]{:S(2)}) async-start(f32[2,8,128]{2,0,1:T(2,128)} %copy.384), calls=%async_computation.4 | async-start | bytes 16384 | tf_op jit(solution)/shard_map/all_to_all | solution.py:141
  194.7 2.1 copy.362
  196.7 2.2 all-to-all-done.3
  199.0 3.6 %all-to-all-start.2 = ((bf16[2,1024,256]{2,0,1:T(2,128)(2,1)}), bf16[2,1024,256]{2,0,1:T(2,128)(2,1)S(1)}, u32[]{:S(2)}, u32[]{:S(2)}) async-start(bf16[2,1024,256]{2,0,1:T(2,128)(2,1)} %copy.362), calls=%async_computation.2 | async-start | bytes 2097152 | tf_op jit(solution)/shard_map/all_to_all | solution.py:140
  204.3 24.8 %all-to-all-done.2 = bf16[2,1024,256]{2,0,1:T(2,128)(2,1)S(1)} async-done(((bf16[2,1024,256]{2,0,1:T(2,128)(2,1)}), bf16[2,1024,256]{2,0,1:T(2,128)(2,1)S(1)}, u32[]{:S(2)}, u32[]{:S(2)}) %all-to-all-start.2) | async-done | bytes 1048608 | tf_op jit(solution)/shard_map/all_to_all | solution.py:140
  229.3 26.3 %reduce-scatter.2.cloned.1.call-done = f32[128,768]{1,0:T(8,128)} async-done(((f32[1024,768]{1,0:T(8,128)}), f32[128,768]{1,0:T(8,128)}) %reduce-scatter.2.cloned.1.call-update) | async-done | bytes 393232 | tf_op jit(solution)/shard_map/reduce_scatter | solution.py:324
  (294 shorter events, 100.2 us)
Async XLA Ops:
  7.2 68.6 %all-gather.2.cloned.1.call-start = ((), (), s32[]{:S(2)}) async-start(), calls=%async_computation.5 | async-start | bytes 1769472 | tf_op jit(solution)/shard_map/all_gather | solution.py:204
  21.6 11.8 %all-to-all-start.1 = ((f32[8,2,128]{2,1,0:T(2,128)}), f32[8,2,128]{2,1,0:T(2,128)S(1)}, u32[]{:S(2)}, u32[]{:S(2)}) async-start(f32[8,2,128]{2,1,0:T(2,128)} %constant_dynamic-update-slice_fusion.3), calls=%async_computation.1 | async-start | bytes 16384 | tf_op jit(solution)/shard_map/all_to_all | solution.py:16
  30.2 7.6 %copy-start.20 = (bf16[128,1024]{1,0:T(8,128)(2,1)S(1)}, bf16[128,1024]{1,0:T(8,128)(2,1)}, u32[]{:S(2)}) copy-start(bf16[128,1024]{1,0:T(8,128)(2,1)} %param.37) | copy-start | bytes 786436
  30.2 7.7 %copy-start.21 = (bf16[128,1024]{1,0:T(8,128)(2,1)S(1)}, bf16[128,1024]{1,0:T(8,128)(2,1)}, u32[]{:S(2)}) copy-start(bf16[128,1024]{1,0:T(8,128)(2,1)} %param.33) | copy-start | bytes 786436
  33.4 42.0 %all-to-all-start = ((bf16[2,128,2048]{1,0,2:T(2,128)(2,1)}), bf16[2,128,2048]{1,0,2:T(2,128)(2,1)S(1)}, u32[]{:S(2)}, u32[]{:S(2)}) async-start(bf16[2,128,2048]{1,0,2:T(2,128)(2,1)} %copy.341), calls=%async_computation | async-start | bytes 2097152 | tf_op jit(solution)/shard_map/all_to_all | solution.py:118
  37.7 217.9 %reduce-scatter.2.cloned.1.call-start = ((), (), s32[]{:S(2)}) async-start(), calls=%async_computation.6 | async-start | bytes 3538944 | tf_op jit(solution)/shard_map/reduce_scatter | solution.py:324
  39.6 35.9 %copy-start.32 = (f32[8]{0:T(128)}, f32[8]{0:T(128)S(1)}, u32[]{:S(2)}) copy-start(f32[8]{0:T(128)S(1)} %convert_reduce_fusion.4) | copy-start | bytes 100
  41.0 34.6 %copy-start.25 = (f32[8,128]{1,0:T(8,128)}, f32[8,128]{1,0:T(8,128)S(1)}, u32[]{:S(2)}) copy-start(f32[8,128]{1,0:T(8,128)S(1)} %get-tuple-element.1394) | copy-start | bytes 12292
  41.2 67.4 %copy-start.22 = (pred[8,128,128]{2,1,0:T(8,128)(4,1)}, pred[8,128,128]{2,1,0:T(8,128)(4,1)S(1)}, u32[]{:S(2)}) copy-start(pred[8,128,128]{2,1,0:T(8,128)(4,1)S(1)} %compare_and_fusion.3) | copy-start | bytes 393220
  42.6 33.0 %copy-start.28 = (f32[8,2]{0,1:T(2,128)}, f32[8,2]{0,1:T(2,128)S(1)}, u32[]{:S(2)}) copy-start(f32[8,2]{0,1:T(2,128)S(1)} %slice_reduce_fusion) | copy-start | bytes 196
  75.7 32.9 %copy-start.10 = (bf16[1,8,128,256]{2,3,1,0:T(8,128)(2,1)}, bf16[1,8,128,256]{2,3,1,0:T(8,128)(2,1)S(1)}, u32[]{:S(2)}) copy-start(bf16[1,8,128,256]{2,3,1,0:T(8,128)(2,1)S(1)} %get-tuple-element.1386) | copy-start | bytes 1572868
  75.7 37.2 %copy-start.1 = (bf16[1,8,128,256]{2,3,1,0:T(8,128)(2,1)}, bf16[1,8,128,256]{2,3,1,0:T(8,128)(2,1)S(1)}, u32[]{:S(2)}) copy-start(bf16[1,8,128,256]{2,3,1,0:T(8,128)(2,1)S(1)} %get-tuple-element.1387) | copy-start | bytes 1572868
  77.3 35.5 %copy-start.6 = (bf16[1024,128]{1,0:T(8,128)(2,1)}, bf16[1024,128]{1,0:T(8,128)(2,1)S(1)}, u32[]{:S(2)}) copy-start(bf16[1024,128]{1,0:T(8,128)(2,1)S(1)} %copy.350) | copy-start | bytes 786436
  77.5 3.5 %copy-start.3 = (bf16[1024,128]{1,0:T(8,128)(2,1)}, bf16[1024,128]{1,0:T(8,128)(2,1)S(1)}, u32[]{:S(2)}) copy-start(bf16[1024,128]{1,0:T(8,128)(2,1)S(1)} %copy.351) | copy-start | bytes 786436
  104.4 4.3 %copy-start.30 = (f32[8,2,128]{2,1,0:T(2,128)S(1)}, f32[8,2,128]{2,1,0:T(2,128)}, u32[]{:S(2)}) copy-start(f32[8,2,128]{2,1,0:T(2,128)} %copy.344) | copy-start | bytes 24580
  105.7 3.0 %copy-start.19 = (f32[8,128,128]{2,1,0:T(8,128)S(1)}, f32[8,128,128]{2,1,0:T(8,128)}, u32[]{:S(2)}) copy-start(f32[8,128,128]{2,1,0:T(8,128)} %fusion.90) | copy-start | bytes 1572868
  136.9 5.6 %copy-start.4 = (bf16[1024,128]{1,0:T(8,128)(2,1)S(1)}, bf16[1024,128]{1,0:T(8,128)(2,1)}, u32[]{:S(2)}) copy-start(bf16[1024,128]{1,0:T(8,128)(2,1)} %copy-done.3) | copy-start | bytes 786436
  140.4 4.6 %copy-start.7 = (bf16[1024,128]{1,0:T(8,128)(2,1)S(1)}, bf16[1024,128]{1,0:T(8,128)(2,1)}, u32[]{:S(2)}) copy-start(bf16[1024,128]{1,0:T(8,128)(2,1)} %copy-done.6) | copy-start | bytes 786436
  142.5 2.5 copy-start.13
  142.5 2.5 copy-start.16
  154.7 4.2 %copy-start.14 = (f32[8,128,128]{2,1,0:T(8,128)S(1)}, f32[8,128,128]{2,1,0:T(8,128)}, u32[]{:S(2)}) copy-start(f32[8,128,128]{2,1,0:T(8,128)} %convolution_add_fusion) | copy-start | bytes 1572868
  162.2 4.0 %copy-start.9 = (f32[8,128,128]{2,1,0:T(8,128)S(1)}, f32[8,128,128]{2,1,0:T(8,128)}, u32[]{:S(2)}) copy-start(f32[8,128,128]{2,1,0:T(8,128)} %copy-done.8) | copy-start | bytes 1572868
  166.2 2.9 %copy-start.11 = (bf16[1,8,128,256]{2,3,1,0:T(8,128)(2,1)S(1)}, bf16[1,8,128,256]{2,3,1,0:T(8,128)(2,1)}, u32[]{:S(2)}) copy-start(bf16[1,8,128,256]{2,3,1,0:T(8,128)(2,1)} %copy-done.10) | copy-start | bytes 1572868
  169.1 4.5 %copy-start.29 = (f32[8,2]{0,1:T(2,128)S(1)}, f32[8,2]{0,1:T(2,128)}, u32[]{:S(2)}) copy-start(f32[8,2]{0,1:T(2,128)} %copy-done.28) | copy-start | bytes 196
  169.1 4.5 %copy-start.33 = (f32[8]{0:T(128)S(1)}, f32[8]{0:T(128)}, u32[]{:S(2)}) copy-start(f32[8]{0:T(128)} %copy-done.32) | copy-start | bytes 100
  169.1 4.6 %copy-start.12 = (f32[8,2,128,128]{3,2,1,0:T(8,128)S(1)}, f32[8,2,128,128]{3,2,1,0:T(8,128)}, u32[]{:S(2)}) copy-start(f32[8,2,128,128]{3,2,1,0:T(8,128)} %get-tuple-element.1401) | copy-start | bytes 3145732
  169.2 4.6 %copy-start.15 = (f32[8,128,128]{1,2,0:T(8,128)S(1)}, f32[8,128,128]{1,2,0:T(8,128)}, u32[]{:S(2)}) copy-start(f32[8,128,128]{1,2,0:T(8,128)} %copy.446) | copy-start | bytes 1572868
  179.8 19.2 %all-to-all-start.3 = ((f32[2,8,128]{2,0,1:T(2,128)}), f32[2,8,128]{2,0,1:T(2,128)S(1)}, u32[]{:S(2)}, u32[]{:S(2)}) async-start(f32[2,8,128]{2,0,1:T(2,128)} %copy.384), calls=%async_computation.4 | async-start | bytes 16384 | tf_op jit(solution)/shard_map/all_to_all | solution.py:141
  194.7 7.9 %copy-start.17 = (bf16[128,2,4,128]{0,3,2,1:T(8,128)(2,1)S(1)}, bf16[128,2,4,128]{0,3,2,1:T(8,128)(2,1)}, u32[]{:S(2)}) copy-start(bf16[128,2,4,128]{0,3,2,1:T(8,128)(2,1)} %get-tuple-element.1371) | copy-start | bytes 786436
  199.0 30.2 %all-to-all-start.2 = ((bf16[2,1024,256]{2,0,1:T(2,128)(2,1)}), bf16[2,1024,256]{2,0,1:T(2,128)(2,1)S(1)}, u32[]{:S(2)}, u32[]{:S(2)}) async-start(bf16[2,1024,256]{2,0,1:T(2,128)(2,1)} %copy.362), calls=%async_computation.2 | async-start | bytes 2097152 | tf_op jit(solution)/shard_map/all_to_all | solution.py:140
  256.5 4.7 %collective-permute-start = (f32[128,256]{1,0:T(8,128)S(1)}, f32[128,256]{1,0:T(8,128)S(1)}, u32[]{:S(2)}, u32[]{:S(2)}) collective-permute-start(f32[128,256]{1,0:T(8,128)S(1)} %slice.80), channel_id=1, source_target_pairs={{0,1},{1,0},{2,3},{3,2},{4,5},{5,4},{6,7},{7,6},{8,9},{9,8},{10,11... | collective-permute-start | bytes 393224 | tf_op jit(solution)/shard_map/ppermute | solution.py:332
  258.0 2.6 copy-start.18
  (11 other events, 15.8 us)
Sparse Core Ops, SparseCore 0:
  11.7 63.4 all-gather.1
  162.3 93.2 reduce-scatter.1
